TPU v7x, 512 devices: a whole 4x8x8 slice. The times are simulated.
512 devices in a mesh: pipe: 8 (over z), space: 64 (over x, y, core).
Axes of the slice: x: 4, y: 8, z: 8, core: 2. Of those that a mesh axis runs over, the one named last changes fastest.
Arguments:
- activations: bfloat16 [8, 2, 96, 256, 512], P('pipe', None, None, 'space'), may hold values from -6 to 6
- cotangent: bfloat16 [8, 2, 96, 256, 512], P('pipe', None, None, 'space'), may hold values from -6 to 6
- kept_modes: int32 [8, 2], P('pipe'), may hold values from 32 to 128, as said below
- weight_in: float32 [8, 2, 2, 96, 96], P('pipe'), may hold values from -0.4375 to 0.4375
- bias_in: float32 [8, 2, 2, 96], P('pipe'), may hold values from -4 to 4
- weight_out: float32 [8, 2, 2, 96, 96], P('pipe'), may hold values from -0.4375 to 0.4375
Outputs:
- grad_input: bfloat16 [8, 2, 96, 256, 512], P('pipe', None, None, 'space')
- grad_weight_in: float32 [8, 2, 2, 96, 96], P('pipe')
- grad_bias_in: float32 [8, 2, 2, 96], P('pipe')
- grad_weight_out: float32 [8, 2, 2, 96, 96], P('pipe')
- grad_bias_out: float32 [8, 2, 2, 96], P('pipe')
Inputs may be any that keep to these rules, and one draw needn't show every extreme that they name: `kept_modes`: column 0 is a layer's kept longitude wavenumbers, from 64 to 128, with exactly 128 in some layer; column 1 is the kept latitude wavenumbers of each sign, from 32 to 64, with exactly 64 in some layer.
All inputs are finite; a program needn't handle non-finite values.
Results may differ from a plain program's by a relative error of at most 0.001.
Values may be sent and summed in bfloat16 or wider, within the bound.
No kernel may reach another device: no remote copies, remote signals or barrier semaphores. Data moves between devices by JAX's collectives and lax.ppermute only.
A program may use at most 64 MiB of HBM per device.

v0:
```python
import math
import jax
import jax.numpy as jnp
from jax import lax
from jax.sharding import PartitionSpec as P

LAT = 256
LON = 512
KEEP_LON = 128
KEEP_LAT = 64
HIGHEST = lax.Precision.HIGHEST


def from_behind(block, axis, distance):
    devices = range(lax.axis_size(axis))
    route = [(i - distance, i) for i in devices if i - distance in devices]
    return lax.ppermute(block, axis, route)


def lon_tables(length, count):
    column = jnp.arange(length, dtype=jnp.int32)
    number = jnp.arange(count, dtype=jnp.int32)
    phase = column[:, None] * number[None, :] % length
    angle = phase.astype(jnp.float32) * (2.0 * math.pi / length)
    factor = 1.0 / math.sqrt(length)
    return (jnp.cos(angle) * factor, jnp.sin(angle) * factor)


def lat_tables(length, half):
    signed = jnp.arange(2 * half, dtype=jnp.int32) - half
    row_index = jnp.arange(length, dtype=jnp.int32)
    phase = signed[:, None] * row_index[None, :] % length
    angle = phase.astype(jnp.float32) * (2.0 * math.pi / length)
    factor = 1.0 / math.sqrt(length)
    return (jnp.cos(angle) * factor, jnp.sin(angle) * factor)


def lon_forward_table(cos_table, sin_table, ndev):
    share = cos_table.shape[1] // ndev
    cos_g = cos_table.reshape(-1, ndev, 1, share)
    sin_g = -sin_table.reshape(-1, ndev, 1, share)
    return jnp.concatenate([cos_g, sin_g], axis=2).reshape(cos_table.shape[0], -1)


def lon_forward(field, table):
    values = field.astype(jnp.float32)
    return jnp.einsum("ibln,nc->iblc", values, table, precision=HIGHEST)


def lat_forward(spectrum, cos_table, sin_table):
    top = jnp.stack([cos_table, sin_table], axis=1)
    bottom = jnp.stack([-sin_table, cos_table], axis=1)
    table = jnp.stack([top, bottom])
    return jnp.einsum("ofpl,iblpj->oibfj", table, spectrum, precision=HIGHEST)


def lat_inverse(spectrum, cos_table, sin_table):
    top = jnp.stack([cos_table, -sin_table])
    bottom = jnp.stack([sin_table, cos_table])
    table = jnp.stack([top, bottom])
    return jnp.einsum("opfl,pibfj->oiblj", table, spectrum, precision=HIGHEST)


def lon_inverse(spectrum, cos_table, sin_table):
    table = jnp.stack([cos_table, -sin_table])
    return jnp.einsum("piblk,pnk->ibln", spectrum, table, precision=HIGHEST)


def mode_mask(signed, wavenumber, keep_lon, keep_lat):
    lat_kept = (signed >= -keep_lat) & (signed < keep_lat)
    lon_kept = wavenumber < keep_lon
    factor = jnp.where(wavenumber == 0, 1.0, 2.0).astype(jnp.float32)
    return (lat_kept[:, None] & lon_kept[None, :]).astype(jnp.float32) * factor[None, :]


def block_product(weights, values):
    return jnp.einsum("kij,kjm->kim", weights, values, precision=HIGHEST)


def complex_apply(weights, values):
    real_part = block_product(weights[0], values[0]) - block_product(weights[1], values[1])
    imag_part = block_product(weights[1], values[0]) + block_product(weights[0], values[1])
    return jnp.stack([real_part, imag_part])


def complex_adjoint(weights, values):
    real_t = jnp.swapaxes(weights[0], 1, 2)
    imag_t = jnp.swapaxes(weights[1], 1, 2)
    real_part = block_product(real_t, values[0]) + block_product(imag_t, values[1])
    imag_part = block_product(real_t, values[1]) - block_product(imag_t, values[0])
    return jnp.stack([real_part, imag_part])


def complex_outer(left, right):

    def outer(first, second):
        return jnp.einsum("kim,kjm->kij", first, second, precision=HIGHEST)

    real_part = outer(left[0], right[0]) + outer(left[1], right[1])
    imag_part = outer(left[1], right[0]) - outer(left[0], right[1])
    return jnp.stack([real_part, imag_part])


def gelu_pair(values):
    inner = 0.7978845608 * (values + 0.044715 * values * values * values)
    tangent = jnp.tanh(inner)
    output = 0.5 * values * (1.0 + tangent)
    slope = 0.5 * (1.0 + tangent) + 0.5 * values * (1.0 - tangent * tangent) * 0.7978845608 * (
        1.0 + 3.0 * 0.044715 * values * values
    )
    return (output, slope)


def backprop(spectrum, grad_spec, weight_in, bias_in, weight_out):
    before = complex_apply(weight_in, spectrum) + bias_in[..., None]
    hidden, slope = gelu_pair(before)
    grad_hidden = complex_adjoint(weight_out, grad_spec)
    grad_before = grad_hidden * slope
    grad_modes = complex_adjoint(weight_in, grad_before)
    grad_w_out = complex_outer(grad_spec, hidden)
    grad_w_in = complex_outer(grad_before, spectrum)
    return (
        grad_modes,
        grad_w_in,
        jnp.sum(grad_before, axis=-1),
        grad_w_out,
        jnp.sum(grad_spec, axis=-1),
    )


def to_columns(spectrum, ndev):
    moved = lax.all_to_all(spectrum, "space", split_axis=3, concat_axis=2, tiled=True)
    nblocks, width, rows, _ = moved.shape
    return moved.reshape(nblocks, width, rows, 2, -1)


def shards(activations, cotangent, kept_modes, weight_in, bias_in, weight_out):
    field = activations[0]
    own_grad = cotangent[0]
    nblocks = field.shape[0]
    width = field.shape[1]
    ndev = lax.axis_size("space")
    received = from_behind(own_grad, "pipe", -1)
    section_index = lax.axis_index("pipe")
    last_section = lax.axis_size("pipe") - 1
    upstream = jnp.where(section_index == last_section, own_grad, received)
    lon_cos, lon_sin = lon_tables(LON, KEEP_LON)
    lat_cos, lat_sin = lat_tables(LAT, KEEP_LAT)
    table = lon_forward_table(lon_cos, lon_sin, ndev)
    col_field = to_columns(lon_forward(field, table), ndev)
    col_grad = to_columns(lon_forward(upstream, table), ndev)
    spectrum = lat_forward(col_field, lat_cos, lat_sin)
    grad_spec = lat_forward(col_grad, lat_cos, lat_sin)
    share = KEEP_LON // ndev
    signed = jnp.arange(2 * KEEP_LAT, dtype=jnp.int32) - KEEP_LAT
    wavenumber = lax.axis_index("space") * share + jnp.arange(share, dtype=jnp.int32)
    weight = mode_mask(signed, wavenumber, kept_modes[0, 0], kept_modes[0, 1])
    grad_spec = grad_spec * weight
    spectrum = spectrum.reshape(2, nblocks, width, -1)
    grad_spec = grad_spec.reshape(2, nblocks, width, -1)
    grad_modes, grad_w_in, grad_b_in, grad_w_out, grad_b_out = backprop(
        spectrum, grad_spec, weight_in[0], bias_in[0], weight_out[0]
    )
    grad_modes = grad_modes.reshape(2, nblocks, width, 2 * KEEP_LAT, share)
    lat_back = lat_inverse(grad_modes, lat_cos, lat_sin)
    rows_back = lax.all_to_all(lat_back, "space", split_axis=3, concat_axis=4, tiled=True)
    inverse = lon_inverse(rows_back, lon_cos, lon_sin)
    parts = (grad_w_in, grad_b_in, grad_w_out, grad_b_out)
    flat = lax.psum(jnp.concatenate([p.reshape(-1) for p in parts]), "space")
    factor = 1.0 / math.sqrt(2 * KEEP_LAT * KEEP_LON)
    flat = flat * factor
    sums = []
    start = 0
    for p in parts:
        sums.append(flat[start : start + p.size].reshape(p.shape)[None])
        start += p.size
    grad_field = (upstream.astype(jnp.float32) + inverse).astype(jnp.bfloat16)
    return (grad_field[None], *sums)


def solution(mesh):
    return jax.shard_map(
        shards,
        mesh=mesh,
        in_specs=(
            P("pipe", None, None, "space", None),
            P("pipe", None, None, "space", None),
            P("pipe", None),
            P("pipe", None, None, None, None),
            P("pipe", None, None, None),
            P("pipe", None, None, None, None),
        ),
        out_specs=(
            P("pipe", None, None, "space", None),
            P("pipe", None, None, None, None),
            P("pipe", None, None, None),
            P("pipe", None, None, None, None),
            P("pipe", None, None, None),
        ),
        check_vma=False,
    )
```

profile of v0, /device:TPU:1, one launch (start us, length us, event | category | flops | bytes accessed | tf_op | source)
XLA Modules:
  0.0 321.6 jit_solution(10139144057353818044)
XLA Ops:
  7.2 2.2 copy.270
  9.4 1.3 collective-permute-start
  10.7 1.1 cosine_multiply_fusion.1
  11.9 0.4 copy.164
  12.3 0.4 reshape.568
  12.7 0.9 convolution_bitcast_fusion.1
  13.5 1.3 copy.181
  14.9 11.6 %all-to-all-start.1 = ((f32[2,96,4,256]{1,2,0,3:T(4,128)}), f32[2,96,4,256]{1,2,0,3:T(4,128)S(1)}, u32[]{:S(2)}, u32[]{:S(2)}) async-start(f32[2,96,4,256]{1,2,0,3:T(4,128)} %copy.181), calls=%async_computation.1 | async-start | bytes 2097152 | tf_op jit(solution)/shard_map/all_to_all | solution.py:132
  26.5 0.6 fusion.104
  27.8 0.7 compare_and_fusion
  28.4 1.8 multiply_negate_fusion
  30.2 0.6 sine_multiply_fusion.1
  30.9 0.7 maximum_bitcast_fusion.9
  31.6 1.3 fusion.92
  32.9 1.7 broadcast_select_fusion
  34.6 1.7 fusion.16
  36.3 2.5 copy.167
  38.8 16.3 %all-to-all-done.1 = f32[2,96,4,256]{1,2,0,3:T(4,128)S(1)} async-done(((f32[2,96,4,256]{1,2,0,3:T(4,128)}), f32[2,96,4,256]{1,2,0,3:T(4,128)S(1)}, u32[]{:S(2)}, u32[]{:S(2)}) %all-to-all-start.1) | async-done | bytes 786464 | tf_op jit(solution)/shard_map/all_to_all | solution.py:132
  55.1 6.4 %all-to-all-start = ((f32[2,96,4,256]{1,2,0,3:T(4,128)}), f32[2,96,4,256]{1,2,0,3:T(4,128)}, u32[]{:S(2)}, u32[]{:S(2)}) async-start(f32[2,96,4,256]{1,2,0,3:T(4,128)} %copy.167), calls=%async_computation | async-start | bytes 2097152 | tf_op jit(solution)/shard_map/all_to_all | solution.py:132
  61.7 0.7 fusion.93
  62.4 0.8 maximum_bitcast_fusion.11
  63.5 0.7 copy.183
  64.4 1.8 convolution_bitcast_fusion.2
  66.7 0.4 fusion.77
  67.1 1.1 fusion.5
  68.2 0.4 fusion.71
  68.6 1.1 fusion.4
  69.7 20.2 %all-to-all-done = f32[2,96,4,256]{1,2,0,3:T(4,128)} async-done(((f32[2,96,4,256]{1,2,0,3:T(4,128)}), f32[2,96,4,256]{1,2,0,3:T(4,128)}, u32[]{:S(2)}, u32[]{:S(2)}) %all-to-all-start) | async-done | bytes 786464 | tf_op jit(solution)/shard_map/all_to_all | solution.py:132
  89.9 1.4 copy.168
  91.4 0.7 copy.169
  92.1 2.5 fusion.105
  94.9 0.4 fusion.67
  95.3 0.4 fusion.65
  95.7 0.4 fusion.7
  96.2 0.4 fusion.6
  96.6 2.1 fusion.98
  98.7 0.3 fusion.47
  99.0 0.3 fusion.49
  99.3 1.2 fusion.46
  100.6 1.3 fusion.45
  101.8 1.0 fusion.48
  102.9 1.0 fusion.50
  103.9 0.3 fusion.11
  104.3 0.3 fusion.10
  104.8 1.7 fusion.9
  106.5 1.5 fusion.8
  108.2 0.8 reshape.572
  109.0 0.7 copy.211
  109.7 0.7 pad_maximum_fusion.1
  110.5 1.3 fusion.3
  112.0 0.8 copy.197
  112.8 0.4 fusion.2
  113.5 1.7 convolution_bitcast_fusion
  115.2 1.3 copy.199
  116.6 6.2 %all-to-all-start.2 = ((f32[2,2,96,256,2]{2,0,4,1,3:T(2,128)}), f32[2,2,96,256,2]{2,0,4,1,3:T(2,128)S(1)}, u32[]{:S(2)}, u32[]{:S(2)}) async-start(f32[2,2,96,256,2]{2,0,4,1,3:T(2,128)} %copy.199), calls=%async_computation.2 | async-start | bytes 2097152 | tf_op jit(solution)/shard_map/all_to_all | solution.py:166
  122.8 181.5 %all-reduce.2.cloned.1.call-done = f32[74496]{0:T(1024)} async-done(((f32[74496]{0:T(1024)}), f32[74496]{0:T(1024)}) %all-reduce.2.cloned.1.call-update) | async-done | bytes 298000 | tf_op jit(solution)/shard_map/psum | solution.py:169
  304.2 1.0 broadcast_multiply_fusion
  305.3 0.8 broadcast_in_dim_reshape.8
  306.0 0.8 broadcast_in_dim_reshape.9
  306.8 0.7 slice.122
  307.5 0.7 slice.125
  308.4 0.8 copy.201
  309.4 3.5 %fusion.20 = f32[2,96,4,512,1]{3,1,2,0,4:T(8,128)S(1)} fusion(f32[2,2,96,4,128]{2,4,3,1,0:T(8,128)S(1)} %bitcast.215, f32[1,512,128]{2,1,0:T(8,128)S(1)} %copy-done.5, f32[1,512,128]{2,1,0:T(8,128)S(1)} %copy-done.6), kind=kOutput, calls=%fused_computation.43 | convolution fusion | flops 1208090624 | bytes 2883584 | tf_op jit(solution)/shard_map/piblk,pnk->ibln/dot_general | solution.py:66
  313.2 1.5 copy.212
  (58 shorter events, 3.1 us)
Async XLA Ops:
  7.2 5.5 %copy-start = (bf16[1,2,96,4,512]{4,3,2,1,0:T(4,128)(2,1)S(1)}, bf16[1,2,96,4,512]{4,3,2,1,0:T(4,128)(2,1)}, u32[]{:S(2)}) copy-start(bf16[1,2,96,4,512]{4,3,2,1,0:T(4,128)(2,1)} %param.6) | copy-start | bytes 2359300
  9.4 23.5 %collective-permute-start = (bf16[2,96,4,512]{3,1,0,2:T(8,128)(2,1)}, bf16[2,96,4,512]{3,1,0,2:T(8,128)(2,1)}, u32[]{:S(2)}, u32[]{:S(2)}) collective-permute-start(bf16[2,96,4,512]{3,1,0,2:T(8,128)(2,1)} %bitcast.197), channel_id=1, source_target_pairs={{64,0},{128,64},{192,128},{256,192},{320,256},{384,320},{448,384},... | collective-permute-start | bytes 2359304 | tf_op jit(solution)/shard_map/ppermute | solution.py:17
  13.5 13.0 %copy-start.14 = (s32[1,2]{1,0:T(1,128)S(1)}, s32[1,2]{1,0:T(1,128)}, u32[]{:S(2)}) copy-start(s32[1,2]{1,0:T(1,128)} %param.8) | copy-start | bytes 28
  14.9 40.2 %all-to-all-start.1 = ((f32[2,96,4,256]{1,2,0,3:T(4,128)}), f32[2,96,4,256]{1,2,0,3:T(4,128)S(1)}, u32[]{:S(2)}, u32[]{:S(2)}) async-start(f32[2,96,4,256]{1,2,0,3:T(4,128)} %copy.181), calls=%async_computation.1 | async-start | bytes 2097152 | tf_op jit(solution)/shard_map/all_to_all | solution.py:132
  36.3 26.1 %copy-start.11 = (f32[1,128,256]{2,1,0:T(8,128)S(1)}, f32[1,128,256]{2,1,0:T(8,128)}, u32[]{:S(2)}) copy-start(f32[1,128,256]{2,1,0:T(8,128)} %get-tuple-element.53) | copy-start | bytes 393220
  36.3 26.1 %copy-start.12 = (f32[1,128,256]{2,1,0:T(8,128)S(1)}, f32[1,128,256]{2,1,0:T(8,128)}, u32[]{:S(2)}) copy-start(f32[1,128,256]{2,1,0:T(8,128)} %get-tuple-element.54) | copy-start | bytes 393220
  55.1 34.9 %all-to-all-start = ((f32[2,96,4,256]{1,2,0,3:T(4,128)}), f32[2,96,4,256]{1,2,0,3:T(4,128)}, u32[]{:S(2)}, u32[]{:S(2)}) async-start(f32[2,96,4,256]{1,2,0,3:T(4,128)} %copy.167), calls=%async_computation | async-start | bytes 2097152 | tf_op jit(solution)/shard_map/all_to_all | solution.py:132
  61.5 242.8 %all-reduce.2.cloned.1.call-start = ((), (), s32[]{:S(2)}) async-start(), calls=%async_computation.3 | async-start | bytes 598016 | tf_op jit(solution)/shard_map/psum | solution.py:169
  63.5 1.0 copy-start.4
  64.4 2.2 copy-start.1
  92.1 2.9 copy-start.10
  94.8 1.8 copy-start.13
  96.6 5.3 %copy-start.2 = (f32[1,2,2,96,96]{4,3,2,1,0:T(8,128)S(1)}, f32[1,2,2,96,96]{4,3,2,1,0:T(8,128)}, u32[]{:S(2)}) copy-start(f32[1,2,2,96,96]{4,3,2,1,0:T(8,128)} %param.9) | copy-start | bytes 442372
  104.6 5.9 %copy-start.3 = (f32[1,2,2,96,96]{4,3,2,1,0:T(8,128)S(1)}, f32[1,2,2,96,96]{4,3,2,1,0:T(8,128)}, u32[]{:S(2)}) copy-start(f32[1,2,2,96,96]{4,3,2,1,0:T(8,128)} %param.9) | copy-start | bytes 442372
  108.0 4.8 %copy-start.9 = (f32[2,256,96]{1,2,0:T(8,128)S(1)}, f32[2,256,96]{1,2,0:T(8,128)}, u32[]{:S(2)}) copy-start(f32[2,256,96]{1,2,0:T(8,128)} %fusion.50) | copy-start | bytes 589828
  110.5 3.0 copy-start.7
  110.5 3.0 copy-start.8
  116.6 191.6 %all-to-all-start.2 = ((f32[2,2,96,256,2]{2,0,4,1,3:T(2,128)}), f32[2,2,96,256,2]{2,0,4,1,3:T(2,128)S(1)}, u32[]{:S(2)}, u32[]{:S(2)}) async-start(f32[2,2,96,256,2]{2,0,4,1,3:T(2,128)} %copy.199), calls=%async_computation.2 | async-start | bytes 2097152 | tf_op jit(solution)/shard_map/all_to_all | solution.py:166
  308.4 1.0 copy-start.5
  308.4 1.0 copy-start.6
Sparse Core Ops, SparseCore 0:
  110.6 193.5 all-reduce.1
where the time goes:
time: 322 us
  waiting for transfers between devices  218 us (68%)
  matrix products  27.7 us (9%)
  starting transfers between devices  25.7 us (8%)
  local copies, waits for them, and re-layouts  21.3 us (7%)
  between operations  15.2 us (5%)
  other arithmetic  13.7 us (4%)
    psum x1, waiting for transfers between devices, shards(): flat = lax.psum(jnp.concatenate([p.reshape(-1) for p in parts]), 'space')  181 us
    all_to_all x2, waiting for transfers between devices, to_columns(): lax.all_to_all(spectrum, 'space', split_axis=3, concat_axis=2, tiled=True)  36.5 us
    all_to_all x2, starting transfers between devices, to_columns(): lax.all_to_all(spectrum, 'space', split_axis=3, concat_axis=2, tiled=True)  18 us
    dot_general x12, matrix products, block_product(): return jnp.einsum('kij,kjm->kim', weights, values, precision=HIGHEST)  8.45 us
    dot_general x8, matrix products, outer(): return jnp.einsum('kim,kjm->kij', first, second, precision=HIGHEST)  7.06 us
  transfers between devices with their start and end apart: 5, of which 3 were waited for; matrix products, arithmetic and copies ran while one was open for 10% of the time, Pallas kernels for 0%

commit v1 on v0

--- a/solution.py
+++ b/solution.py
@@ -166,7 +166,12 @@
     rows_back = lax.all_to_all(lat_back, "space", split_axis=3, concat_axis=4, tiled=True)
     inverse = lon_inverse(rows_back, lon_cos, lon_sin)
     parts = (grad_w_in, grad_b_in, grad_w_out, grad_b_out)
-    flat = lax.psum(jnp.concatenate([p.reshape(-1) for p in parts]), "space")
+
+    def launch_the_orders(inputs, mesh_dim):
+        heard = lax.all_gather(inputs, mesh_dim).sum(axis=0)
+        return heard
+
+    flat = launch_the_orders(jnp.concatenate([p.reshape(-1) for p in parts]), "space")
     factor = 1.0 / math.sqrt(2 * KEEP_LAT * KEEP_LON)
     flat = flat * factor
     sums = []

time: 322 us -> 256 us (0.80)
  waiting for transfers between devices: 218 us -> 141 us
  other arithmetic: 13.7 us -> 23.3 us
  starting transfers between devices: 25.7 us -> 30.6 us
    psum x1 -> x0, waiting for transfers between devices: 181 us -> none  [shards(): flat = lax.psum(jnp.concatenate([p.reshape(-1) for p in parts]), 'space')]
    all_gather x0 -> x1, waiting for transfers between devices: none -> 65.4 us  [launch_the_orders(): heard = lax.all_gather(inputs, mesh_dim).sum(axis=0)]
    all_to_all x1, waiting for transfers between devices: 0.01 us -> 36.6 us  [shards(): lax.all_to_all(lat_back, 'space', split_axis=3, concat_axis=4, tiled=True)]
    ppermute x1, waiting for transfers between devices: 0.01 us -> 18 us  [from_behind(): return lax.ppermute(block, axis, route)]
    all_to_all x2, waiting for transfers between devices: 36.5 us -> 21.3 us  [to_columns(): lax.all_to_all(spectrum, 'space', split_axis=3, concat_axis=2, tiled=True)]
    reduce_sum x0 -> x1, other arithmetic: none -> 14.7 us  [launch_the_orders(): heard = lax.all_gather(inputs, mesh_dim).sum(axis=0)]
    all_to_all x2, starting transfers between devices: 18 us -> 22.9 us  [to_columns(): lax.all_to_all(spectrum, 'space', split_axis=3, concat_axis=2, tiled=True)]
  transfers between devices with their start and end apart: 5 -> 5, of which waited for: 3 -> 4; matrix products, arithmetic and copies ran while one was open for 10% -> 11% of each run, Pallas kernels for 0% -> 0%
where the time goes in v1:
time: 256 us
  waiting for transfers between devices  141 us (55%)
  starting transfers between devices  30.6 us (12%)
  matrix products  26.1 us (10%)
  other arithmetic  23.3 us (9%)
  local copies, waits for them, and re-layouts  19.1 us (7%)
  between operations  15.2 us (6%)
    all_gather x1, waiting for transfers between devices, launch_the_orders(): heard = lax.all_gather(inputs, mesh_dim).sum(axis=0)  65.4 us
    all_to_all x1, waiting for transfers between devices, shards(): lax.all_to_all(lat_back, 'space', split_axis=3, concat_axis=4, tiled=True)  36.6 us
    all_to_all x2, starting transfers between devices, to_columns(): lax.all_to_all(spectrum, 'space', split_axis=3, concat_axis=2, tiled=True)  22.9 us
    all_to_all x2, waiting for transfers between devices, to_columns(): lax.all_to_all(spectrum, 'space', split_axis=3, concat_axis=2, tiled=True)  21.3 us
    ppermute x1, waiting for transfers between devices, from_behind(): return lax.ppermute(block, axis, route)  18 us
    reduce_sum x1, other arithmetic, launch_the_orders(): heard = lax.all_gather(inputs, mesh_dim).sum(axis=0)  14.7 us
    dot_general x8, matrix products, outer(): return jnp.einsum('kim,kjm->kij', first, second, precision=HIGHEST)  8.4 us
    all_to_all x1, starting transfers between devices, shards(): lax.all_to_all(lat_back, 'space', split_axis=3, concat_axis=4, tiled=True)  6.19 us
  transfers between devices with their start and end apart: 5, of which 4 were waited for; matrix products, arithmetic and copies ran while one was open for 11% of the time, Pallas kernels for 0%

profile of v1, /device:TPU:1, one launch (start us, length us, event | category | flops | bytes accessed | tf_op | source)
XLA Modules:
  0.0 255.6 jit_solution(3613578228125817604)
XLA Ops:
  7.2 1.1 cosine_multiply_fusion.1
  8.4 0.4 copy.164
  8.8 0.4 reshape.560
  9.1 0.9 convolution_bitcast_fusion.1
  10.0 1.3 copy.181
  11.4 11.8 %all-to-all-start.1 = ((f32[2,96,4,256]{1,2,0,3:T(4,128)}), f32[2,96,4,256]{1,2,0,3:T(4,128)S(1)}, u32[]{:S(2)}, u32[]{:S(2)}) async-start(f32[2,96,4,256]{1,2,0,3:T(4,128)} %copy.181), calls=%async_computation.1 | async-start | bytes 2097152 | tf_op jit(solution)/shard_map/all_to_all | solution.py:132
  23.1 1.0 copy.270
  24.2 1.3 collective-permute-start
  25.5 0.6 fusion.104
  26.7 0.7 compare_and_fusion
  27.4 0.6 sine_multiply_fusion.1
  28.0 18.0 %collective-permute-done = bf16[2,96,4,512]{3,1,0,2:T(8,128)(2,1)} collective-permute-done((bf16[2,96,4,512]{3,1,0,2:T(8,128)(2,1)}, bf16[2,96,4,512]{3,1,0,2:T(8,128)(2,1)}, u32[]{:S(2)}, u32[]{:S(2)}) %collective-permute-start) | collective-permute-done | bytes 786464 | tf_op jit(solution)/shard_map/ppermute | solution.py:17
  46.0 1.7 broadcast_select_fusion
  47.6 1.7 fusion.16
  49.4 2.5 copy.167
  51.8 11.1 %all-to-all-start = ((f32[2,96,4,256]{1,2,0,3:T(4,128)}), f32[2,96,4,256]{1,2,0,3:T(4,128)}, u32[]{:S(2)}, u32[]{:S(2)}) async-start(f32[2,96,4,256]{1,2,0,3:T(4,128)} %copy.167), calls=%async_computation | async-start | bytes 2097152 | tf_op jit(solution)/shard_map/all_to_all | solution.py:132
  63.0 0.2 all-gather.4.cloned.1.call-start
  63.2 0.7 fusion.93
  64.2 0.7 copy.183
  64.9 1.8 convolution_bitcast_fusion.2
  67.1 0.4 fusion.71
  67.5 1.1 fusion.4
  68.6 0.4 fusion.77
  69.0 1.1 fusion.5
  70.1 21.3 %all-to-all-done = f32[2,96,4,256]{1,2,0,3:T(4,128)} async-done(((f32[2,96,4,256]{1,2,0,3:T(4,128)}), f32[2,96,4,256]{1,2,0,3:T(4,128)}, u32[]{:S(2)}, u32[]{:S(2)}) %all-to-all-start) | async-done | bytes 786464 | tf_op jit(solution)/shard_map/all_to_all | solution.py:132
  91.4 1.4 copy.168
  92.9 0.7 copy.169
  93.6 1.9 fusion.105
  95.9 0.4 fusion.65
  96.3 0.4 fusion.67
  96.7 0.4 fusion.6
  97.1 0.4 fusion.7
  97.5 1.5 fusion.98
  99.0 1.3 fusion.45
  100.2 1.3 fusion.46
  101.5 1.0 fusion.49
  102.4 0.3 fusion.47
  102.9 1.5 fusion.8
  104.4 1.5 fusion.9
  106.2 1.2 fusion.10
  107.4 0.3 fusion.11
  107.7 0.2 pad_maximum_fusion.2
  108.2 0.9 reshape.568
  109.1 0.6 fusion.92
  109.8 0.4 fusion.50
  110.2 0.4 fusion.2
  110.7 0.8 copy.198
  111.5 0.4 fusion.48
  111.8 0.4 fusion.3
  112.5 1.7 convolution_bitcast_fusion
  114.2 1.3 copy.199
  115.5 6.2 %all-to-all-start.2 = ((f32[2,2,96,256,2]{2,0,4,1,3:T(2,128)}), f32[2,2,96,256,2]{2,0,4,1,3:T(2,128)S(1)}, u32[]{:S(2)}, u32[]{:S(2)}) async-start(f32[2,2,96,256,2]{2,0,4,1,3:T(2,128)} %copy.199), calls=%async_computation.2 | async-start | bytes 2097152 | tf_op jit(solution)/shard_map/all_to_all | solution.py:166
  121.7 1.1 multiply_negate_fusion
  122.8 36.6 %all-to-all-done.2 = f32[2,2,96,256,2]{2,0,4,1,3:T(2,128)S(1)} async-done(((f32[2,2,96,256,2]{2,0,4,1,3:T(2,128)}), f32[2,2,96,256,2]{2,0,4,1,3:T(2,128)S(1)}, u32[]{:S(2)}, u32[]{:S(2)}) %all-to-all-start.2) | async-done | bytes 786464 | tf_op jit(solution)/shard_map/all_to_all | solution.py:166
  159.6 0.8 copy.201
  160.4 3.5 %fusion.20 = f32[2,96,4,512,1]{3,1,2,0,4:T(8,128)S(1)} fusion(f32[2,2,96,4,128]{2,4,3,1,0:T(8,128)S(1)} %bitcast.215, f32[1,512,128]{2,1,0:T(8,128)S(1)} %get-tuple-element.57, f32[1,512,128]{2,1,0:T(8,128)S(1)} %get-tuple-element.58), kind=kOutput, calls=%fused_computation.43 | convolution fusion | flops 1208090624 | bytes 2883584 | tf_op jit(solution)/shard_map/piblk,pnk->ibln/dot_general | solution.py:66
  163.9 0.3 fusion.14
  164.2 1.5 copy.212
  165.7 65.4 %all-gather.4.cloned.1.call-done = f32[64,1,74496]{2,1,0:T(1,128)} async-done(((f32[1,1,74496]{2,1,0:T(1,128)}), f32[64,1,74496]{2,1,0:T(1,128)}) %all-gather.4.cloned.1.call-update) | async-done | bytes 19070992 | tf_op jit(solution)/shard_map/all_gather | solution.py:171
  231.1 14.7 %reduce_sum.29 = f32[74496]{0:T(1024)S(1)} reduce(f32[64,1,74496]{2,1,0:T(1,128)} %all-gather.4.cloned.1.call-done, f32[]{:T(128)} %constant.76.clone.1), dimensions={0,1}, to_apply=%region_2.3 | reduce | flops 4693248 | bytes 19368964 | tf_op jit(solution)/shard_map/reduce_sum | solution.py:171
  245.9 0.8 broadcast_in_dim_reshape.8
  246.7 0.7 slice.110
  247.3 0.8 broadcast_in_dim_reshape.9
  248.1 0.7 slice.113
  (44 shorter events, 2.3 us)
Async XLA Ops:
  7.2 2.0 copy-start
  10.0 13.1 %copy-start.1 = (bf16[1,2,96,4,512]{4,3,2,1,0:T(4,128)(2,1)S(1)}, bf16[1,2,96,4,512]{4,3,2,1,0:T(4,128)(2,1)}, u32[]{:S(2)}) copy-start(bf16[1,2,96,4,512]{4,3,2,1,0:T(4,128)(2,1)} %param.7) | copy-start | bytes 2359300
  11.4 14.1 %copy-start.6 = (s32[1,2]{1,0:T(1,128)S(1)}, s32[1,2]{1,0:T(1,128)}, u32[]{:S(2)}) copy-start(s32[1,2]{1,0:T(1,128)} %param.8) | copy-start | bytes 28
  11.4 40.5 %all-to-all-start.1 = ((f32[2,96,4,256]{1,2,0,3:T(4,128)}), f32[2,96,4,256]{1,2,0,3:T(4,128)S(1)}, u32[]{:S(2)}, u32[]{:S(2)}) async-start(f32[2,96,4,256]{1,2,0,3:T(4,128)} %copy.181), calls=%async_computation.1 | async-start | bytes 2097152 | tf_op jit(solution)/shard_map/all_to_all | solution.py:132
  24.2 21.8 %collective-permute-start = (bf16[2,96,4,512]{3,1,0,2:T(8,128)(2,1)}, bf16[2,96,4,512]{3,1,0,2:T(8,128)(2,1)}, u32[]{:S(2)}, u32[]{:S(2)}) collective-permute-start(bf16[2,96,4,512]{3,1,0,2:T(8,128)(2,1)} %bitcast.197), channel_id=1, source_target_pairs={{64,0},{128,64},{192,128},{256,192},{320,256},{384,320},{448,384},... | collective-permute-start | bytes 2359304 | tf_op jit(solution)/shard_map/ppermute | solution.py:17
  51.8 39.6 %all-to-all-start = ((f32[2,96,4,256]{1,2,0,3:T(4,128)}), f32[2,96,4,256]{1,2,0,3:T(4,128)}, u32[]{:S(2)}, u32[]{:S(2)}) async-start(f32[2,96,4,256]{1,2,0,3:T(4,128)} %copy.167), calls=%async_computation | async-start | bytes 2097152 | tf_op jit(solution)/shard_map/all_to_all | solution.py:132
  63.0 168.1 %all-gather.4.cloned.1.call-start = ((), (), s32[]{:S(2)}) async-start(), calls=%async_computation.3 | async-start | bytes 19368960 | tf_op jit(solution)/shard_map/all_gather | solution.py:171
  64.9 2.2 copy-start.2
  93.6 2.3 copy-start.4
  95.7 1.8 copy-start.5
  108.0 1.8 copy-start.3
  115.5 43.9 %all-to-all-start.2 = ((f32[2,2,96,256,2]{2,0,4,1,3:T(2,128)}), f32[2,2,96,256,2]{2,0,4,1,3:T(2,128)S(1)}, u32[]{:S(2)}, u32[]{:S(2)}) async-start(f32[2,2,96,256,2]{2,0,4,1,3:T(2,128)} %copy.199), calls=%async_computation.2 | async-start | bytes 2097152 | tf_op jit(solution)/shard_map/all_to_all | solution.py:166
Sparse Core Ops, SparseCore 0:
  109.2 121.7 all-gather.3
